TPU v7x, 512 devices: a whole 4x4x16 slice. The times are simulated.
512 devices in a mesh: tile: 128 (over z, y_hi, x), lev: 4 (over y_lo, core).
Axes of the slice: x: 4, y: 4 (y_hi: 2, y_lo: 2; y = y_hi * 2 + y_lo), z: 16, core: 2. Of those that a mesh axis runs over, the one named last changes fastest.
Arguments:
- forcing: float32 [2, 52, 6144, 128], P(None, 'lev', 'tile'), may hold values from -6 to 6
- lateral_mix: float32 [52], P('lev'), may hold values from 0.05 to 0.15
- sea_mask: int32 [6144, 128], P('tile'), may hold values 0 or 1
- convective: int32 [6144, 128], P('tile'), may hold values 0 or 1
- mixing_inverse: float32 [2, 2, 52, 52], replicated, may hold values from -1.5 to 1.5
- seam_links: int32 [128, 8], P('tile'), may hold values from 0 to 511, as said below
Outputs:
- swept: float32 [2, 52, 6144, 128], P(None, 'lev', 'tile')
Inputs may be any that keep to these rules, and one draw needn't show every extreme that they name: Tile t sits at row t // 16 and column t % (16) of a grid of 8 rows that closes in both directions. seam_links[t, k] = 4 * s + code, where s is the tile beside t in that grid toward the previous row (k = 0), the next row (k = 1), the previous column (k = 2), the next column (k = 3), and diagonally (k = 4: previous row and column, 5: previous row and next column, 6: next row and previous column, 7: next row and next column).
All inputs are finite; a program needn't handle non-finite values. No bound on the sum of `sea_mask` or of `convective` on one device may be relied on, other than what follows from the above.
Results may differ from a plain program's by a relative error of at most 0.0001.
Values sent between devices are 32-bit elements; how exact they have to be, the bound alone decides.
No kernel may reach another device: no remote copies, remote signals or barrier semaphores. Data moves between devices by JAX's collectives and lax.ppermute only.
A program may use at most 64 MiB of HBM per device.

v0:
```python
import jax
import jax.numpy as jnp
from jax import lax
from jax.sharding import PartitionSpec as P

STEPS = 2
SLOT_STEPS = ((-1, 0), (1, 0), (0, -1), (0, 1), (-1, -1), (-1, 1), (1, -1), (1, 1))


def passed_along(value, axis, steps):
    count = lax.axis_size(axis)
    pairs = [(source, (source + steps) % count) for source in range(count)]
    return lax.ppermute(value, axis, pairs)


def strip_set(field):
    return jnp.concatenate(
        [
            field[..., 0, :],
            field[..., -1, :],
            field[..., :, 0],
            field[..., :, -1],
            field[..., 0, 0:1],
            field[..., 0, -1:],
            field[..., -1, 0:1],
            field[..., -1, -1:],
        ],
        axis=-1,
    )


def assemble(field, south, north, west, east, corners):
    middle = jnp.concatenate([west[..., None], field, east[..., None]], axis=-1)
    top_row = jnp.concatenate([corners[0][..., None], south, corners[1][..., None]], axis=-1)
    bottom_row = jnp.concatenate([corners[2][..., None], north, corners[3][..., None]], axis=-1)
    return jnp.concatenate([top_row[..., None, :], middle, bottom_row[..., None, :]], axis=-2)


def stencil(extended, field, rate, wet):
    edge_sum = (
        extended[..., :-2, 1:-1]
        + extended[..., 2:, 1:-1]
        + extended[..., 1:-1, :-2]
        + extended[..., 1:-1, 2:]
    )
    diag_sum = (
        extended[..., :-2, :-2]
        + extended[..., :-2, 2:]
        + extended[..., 2:, :-2]
        + extended[..., 2:, 2:]
    )
    return wet * ((1.0 - 6.0 * rate) * field + rate * edge_sum + 0.5 * rate * diag_sum)


def offset_slots(width, count):
    listing = {}
    for column in range(width):
        for slot in range(8):
            row_move, col_move = SLOT_STEPS[slot]
            moved_by = row_move * width + (column + col_move) % width - column
            distance = -moved_by % count
            if distance not in listing:
                listing[distance] = []
            listing[distance].append(slot)
    return listing


def seam_select(own_strips, seam_links):
    tile_count = lax.axis_size("tile")
    listing = offset_slots(tile_count // 8, tile_count)
    offsets = sorted(listing)
    received = []
    for shift_by in offsets:
        filled = passed_along(own_strips, "tile", shift_by)
        received.append(filled)
    stacked = jnp.stack(received)
    tile_here = lax.axis_index("tile")
    source = seam_links[0] // 4
    codes = seam_links[0] % 4
    distance = (tile_here - source) % tile_count
    offset_table = jnp.array(offsets, jnp.int32)
    selector = (distance[:, None] == offset_table[None, :]).astype(jnp.float32)
    chosen = jnp.einsum("sk,ktlp->stlp", selector, stacked, precision=lax.Precision.HIGHEST)
    return (chosen, codes)


def level_horizontal(adjoint, lateral_mix, wet, seam_links):
    rows = adjoint.shape[2]
    cols = adjoint.shape[3]
    chosen, codes = seam_select(strip_set(adjoint), seam_links)

    def edge(slot, first, last, length):
        part_a = chosen[slot][:, :, first : first + length]
        part_b = chosen[slot][:, :, last : last + length]
        strip = jnp.where(codes[slot] % 2 == 0, part_a, part_b)
        return jnp.where(codes[slot] // 2 == 1, strip[..., ::-1], strip)

    base = 2 * cols + 2 * rows

    def corner(slot):
        return lax.dynamic_index_in_dim(chosen[slot], base + codes[slot], axis=2, keepdims=False)

    south = edge(0, 0, cols, cols)
    north = edge(1, 0, cols, cols)
    west = edge(2, 2 * cols, 2 * cols + rows, rows)
    east = edge(3, 2 * cols, 2 * cols + rows, rows)
    corners = [corner(4), corner(5), corner(6), corner(7)]
    extended = assemble(adjoint, south, north, west, east, corners)
    rate = lateral_mix[None, :, None, None]
    return stencil(extended, adjoint, rate, wet[None, None])


def local(forcing, lateral_mix, sea_mask, convective, mixing_inverse, seam_links):
    wet = sea_mask.astype(jnp.float32)
    depth = forcing.shape[1]
    lev_here = lax.axis_index("lev")
    adjoint = forcing
    for step in range(STEPS):
        lateral = level_horizontal(adjoint, lateral_mix, wet, seam_links)
        own_levels = lax.dynamic_slice_in_dim(mixing_inverse, lev_here * depth, depth, axis=3)
        both_states = jnp.einsum(
            "tsml,tmxy->tslxy",
            own_levels,
            lax.all_gather(lateral, "lev", axis=1, tiled=True),
            precision=lax.Precision.HIGHEST,
        )
        adjoint = jnp.where(convective[None, None] == 1, both_states[:, 1], both_states[:, 0])
    return adjoint


def solution(mesh):
    return jax.shard_map(
        local,
        mesh=mesh,
        in_specs=(
            P(None, "lev", "tile", None),
            P("lev"),
            P("tile", None),
            P("tile", None),
            P(),
            P("tile", None),
        ),
        out_specs=P(None, "lev", "tile", None),
        check_vma=False,
    )
```

profile of v0, /device:TPU:1, one launch (start us, length us, event | category | flops | bytes accessed | tf_op | source)
XLA Modules:
  0.0 261.6 jit_solution(10945361443010133119)
XLA Ops:
  6.5 1.0 fusion.37
  7.5 1.4 slice_reduce_fusion
  8.9 1.6 fusion.36
  10.6 0.1 copy.873
  10.7 0.1 copy.874
  10.8 0.1 copy.875
  11.0 0.3 copy.871
  11.3 0.3 copy.872
  11.6 0.2 concatenate.58
  11.8 3.9 %collective-permute-start = (f32[2,13,356]{2,0,1:T(2,128)S(1)}, f32[2,13,356]{2,0,1:T(2,128)S(1)}, u32[]{:S(2)}, u32[]{:S(2)}) collective-permute-start(f32[2,13,356]{2,0,1:T(2,128)S(1)} %concatenate.58), channel_id=1, source_target_pairs={{0,4},{4,8},{8,12},{12,16},{16,20},{20,24},{24,28},{28,32},{32,36}... | collective-permute-start | bytes 111080 | tf_op jit(solution)/shard_map/ppermute | solution.py:13
  15.7 8.5 %collective-permute-start.1 = (f32[2,13,356]{2,0,1:T(2,128)S(1)}, f32[2,13,356]{2,0,1:T(2,128)S(1)}, u32[]{:S(2)}, u32[]{:S(2)}) collective-permute-start(f32[2,13,356]{2,0,1:T(2,128)S(1)} %concatenate.58), channel_id=1, source_target_pairs={{0,60},{4,64},{8,68},{12,72},{16,76},{20,80},{24,84},{28,88},{32,9... | collective-permute-start | bytes 111080 | tf_op jit(solution)/shard_map/ppermute | solution.py:13
  24.2 6.1 %collective-permute-start.2 = (f32[2,13,356]{2,0,1:T(2,128)S(1)}, f32[2,13,356]{2,0,1:T(2,128)S(1)}, u32[]{:S(2)}, u32[]{:S(2)}) collective-permute-start(f32[2,13,356]{2,0,1:T(2,128)S(1)} %concatenate.58), channel_id=1, source_target_pairs={{0,64},{4,68},{8,72},{12,76},{16,80},{20,84},{24,88},{28,92},{32,9... | collective-permute-start | bytes 111080 | tf_op jit(solution)/shard_map/ppermute | solution.py:13
  30.4 2.2 collective-permute-start.3
  32.6 14.2 %collective-permute-start.4 = (f32[2,13,356]{2,0,1:T(2,128)S(1)}, f32[2,13,356]{2,0,1:T(2,128)S(1)}, u32[]{:S(2)}, u32[]{:S(2)}) collective-permute-start(f32[2,13,356]{2,0,1:T(2,128)S(1)} %concatenate.58), channel_id=1, source_target_pairs={{0,124},{4,128},{8,132},{12,136},{16,140},{20,144},{24,148},{28,15... | collective-permute-start | bytes 111080 | tf_op jit(solution)/shard_map/ppermute | solution.py:13
  46.9 1.9 collective-permute-start.5
  48.8 7.3 %collective-permute-start.6 = (f32[2,13,356]{2,0,1:T(2,128)S(1)}, f32[2,13,356]{2,0,1:T(2,128)S(1)}, u32[]{:S(2)}, u32[]{:S(2)}) collective-permute-start(f32[2,13,356]{2,0,1:T(2,128)S(1)} %concatenate.58), channel_id=1, source_target_pairs={{0,444},{4,448},{8,452},{12,456},{16,460},{20,464},{24,468},{28,47... | collective-permute-start | bytes 111080 | tf_op jit(solution)/shard_map/ppermute | solution.py:13
  56.1 4.0 %collective-permute-start.7 = (f32[2,13,356]{2,0,1:T(2,128)S(1)}, f32[2,13,356]{2,0,1:T(2,128)S(1)}, u32[]{:S(2)}, u32[]{:S(2)}) collective-permute-start(f32[2,13,356]{2,0,1:T(2,128)S(1)} %concatenate.58), channel_id=1, source_target_pairs={{0,448},{4,452},{8,456},{12,460},{16,464},{20,468},{24,472},{28,47... | collective-permute-start | bytes 111080 | tf_op jit(solution)/shard_map/ppermute | solution.py:13
  60.1 1.9 collective-permute-start.8
  62.0 10.3 %collective-permute-start.9 = (f32[2,13,356]{2,0,1:T(2,128)S(1)}, f32[2,13,356]{2,0,1:T(2,128)S(1)}, u32[]{:S(2)}, u32[]{:S(2)}) collective-permute-start(f32[2,13,356]{2,0,1:T(2,128)S(1)} %concatenate.58), channel_id=1, source_target_pairs={{0,508},{4,0},{8,4},{12,8},{16,12},{20,16},{24,20},{28,24},{32,28}... | collective-permute-start | bytes 111080 | tf_op jit(solution)/shard_map/ppermute | solution.py:13
  72.3 0.7 fusion.42
  88.1 0.2 copy.868
  89.1 0.8 stack.76
  89.9 0.4 fusion.26
  90.3 0.2 fusion.39
  91.3 0.1 rev.25
  91.5 0.4 copy.894
  92.1 0.1 rev.26
  92.3 0.4 copy.896
  92.9 1.3 maximum_maximum_fusion
  94.2 1.5 fusion.16
  95.8 1.0 copy.906
  96.8 0.2 all-gather.5.cloned.1.call-start
  97.1 0.2 constant_dynamic-slice_fusion.8
  97.2 0.1 copy.953
  97.4 38.6 %all-gather.3.cloned.1.call-done = f32[2,52,48,128]{3,2,0,1:T(8,128)} async-done(((f32[2,13,48,128]{3,2,0,1:T(8,128)}), f32[2,52,48,128]{3,2,0,1:T(8,128)}) %all-gather.3.cloned.1.call-update) | async-done | bytes 2555920 | tf_op jit(solution)/shard_map/all_gather | solution.py:124
  135.9 4.8 %fusion.2 = f32[2,2,13,48,128]{4,2,3,1,0:T(8,128)S(1)} fusion(f32[2,52,48,128,1]{3,2,0,1,4:T(8,128)} %bitcast.191, f32[2,2,52,13]{2,3,1,0:T(8,128)S(1)} %copy.953), kind=kOutput, calls=%fused_computation.2 | convolution fusion | flops 199360512 | bytes 3844672 | tf_op jit(solution)/shard_map/tsml,tmxy->tslxy/dot_general | solution.py:121
  140.8 0.1 fusion.13
  140.9 0.3 fusion.35
  141.2 0.4 copy.910
  141.6 0.3 copy.911
  142.0 3.1 %collective-permute-start.10 = (f32[2,13,356]{2,1,0:T(8,128)S(1)}, f32[2,13,356]{2,1,0:T(8,128)S(1)}, u32[]{:S(2)}, u32[]{:S(2)}) collective-permute-start(f32[2,13,356]{2,1,0:T(8,128)S(1)} %concatenate.66), channel_id=1, source_target_pairs={{0,4},{4,8},{8,12},{12,16},{16,20},{20,24},{24,28},{28,32},{32,36}... | collective-permute-start | bytes 111080 | tf_op jit(solution)/shard_map/ppermute | solution.py:13
  145.1 7.8 %collective-permute-start.11 = (f32[2,13,356]{2,1,0:T(8,128)S(1)}, f32[2,13,356]{2,1,0:T(8,128)S(1)}, u32[]{:S(2)}, u32[]{:S(2)}) collective-permute-start(f32[2,13,356]{2,1,0:T(8,128)S(1)} %concatenate.66), channel_id=1, source_target_pairs={{0,60},{4,64},{8,68},{12,72},{16,76},{20,80},{24,84},{28,88},{32,9... | collective-permute-start | bytes 111080 | tf_op jit(solution)/shard_map/ppermute | solution.py:13
  152.9 5.4 %collective-permute-start.12 = (f32[2,13,356]{2,1,0:T(8,128)S(1)}, f32[2,13,356]{2,1,0:T(8,128)S(1)}, u32[]{:S(2)}, u32[]{:S(2)}) collective-permute-start(f32[2,13,356]{2,1,0:T(8,128)S(1)} %concatenate.66), channel_id=1, source_target_pairs={{0,64},{4,68},{8,72},{12,76},{16,80},{20,84},{24,88},{28,92},{32,9... | collective-permute-start | bytes 111080 | tf_op jit(solution)/shard_map/ppermute | solution.py:13
  158.3 1.9 collective-permute-start.13
  160.2 12.3 %collective-permute-start.14 = (f32[2,13,356]{2,1,0:T(8,128)S(1)}, f32[2,13,356]{2,1,0:T(8,128)S(1)}, u32[]{:S(2)}, u32[]{:S(2)}) collective-permute-start(f32[2,13,356]{2,1,0:T(8,128)S(1)} %concatenate.66), channel_id=1, source_target_pairs={{0,124},{4,128},{8,132},{12,136},{16,140},{20,144},{24,148},{28,15... | collective-permute-start | bytes 111080 | tf_op jit(solution)/shard_map/ppermute | solution.py:13
  172.6 1.9 collective-permute-start.15
  174.5 9.4 %collective-permute-start.16 = (f32[2,13,356]{2,1,0:T(8,128)S(1)}, f32[2,13,356]{2,1,0:T(8,128)S(1)}, u32[]{:S(2)}, u32[]{:S(2)}) collective-permute-start(f32[2,13,356]{2,1,0:T(8,128)S(1)} %concatenate.66), channel_id=1, source_target_pairs={{0,444},{4,448},{8,452},{12,456},{16,460},{20,464},{24,468},{28,47... | collective-permute-start | bytes 111080 | tf_op jit(solution)/shard_map/ppermute | solution.py:13
  184.0 1.9 collective-permute-start.17
  186.0 1.9 collective-permute-start.18
  187.9 8.1 %collective-permute-start.19 = (f32[2,13,356]{2,1,0:T(8,128)S(1)}, f32[2,13,356]{2,1,0:T(8,128)S(1)}, u32[]{:S(2)}, u32[]{:S(2)}) collective-permute-start(f32[2,13,356]{2,1,0:T(8,128)S(1)} %concatenate.66), channel_id=1, source_target_pairs={{0,508},{4,0},{8,4},{12,8},{16,12},{20,16},{24,20},{28,24},{32,28}... | collective-permute-start | bytes 111080 | tf_op jit(solution)/shard_map/ppermute | solution.py:13
  196.2 0.8 collective-permute-done.19
  197.0 0.6 fusion.21
  197.5 0.2 fusion.38
  198.5 0.1 rev.29
  198.7 0.4 copy.924
  199.3 0.1 rev.30
  199.5 0.4 copy.925
  200.1 1.3 maximum_maximum_fusion.1
  201.4 1.5 fusion.8
  202.9 1.0 copy.933
  204.0 44.8 %all-gather.5.cloned.1.call-done = f32[2,52,48,128]{3,2,0,1:T(8,128)} async-done(((f32[2,13,48,128]{3,2,0,1:T(8,128)}), f32[2,52,48,128]{3,2,0,1:T(8,128)}) %all-gather.5.cloned.1.call-update) | async-done | bytes 2555920 | tf_op jit(solution)/shard_map/all_gather | solution.py:124
  248.8 4.8 %fusion = f32[2,2,13,48,128]{4,2,3,0,1:T(8,128)S(1)} fusion(f32[2,52,48,128]{3,2,0,1:T(8,128)} %all-gather.5.cloned.1.call-done, f32[2,2,52,13]{2,3,1,0:T(8,128)S(1)} %copy.953), kind=kOutput, calls=%fused_computation | convolution fusion | flops 199360512 | bytes 3844672 | tf_op jit(solution)/shard_map/tsml,tmxy->tslxy/dot_general | solution.py:121
  253.6 0.1 fusion.5
  253.7 1.0 copy.937
  (117 shorter events, 3.2 us)
Async XLA Ops:
  6.5 90.5 %copy-start = (f32[2,2,52,52]{3,1,2,0:T(2,128)S(1)}, f32[2,2,52,52]{3,1,2,0:T(2,128)}, u32[]{:S(2)}) copy-start(f32[2,2,52,52]{3,1,2,0:T(2,128)} %param.12) | copy-start | bytes 129796
  6.5 129.4 %all-gather.3.cloned.1.call-start = ((), (), s32[]{:S(2)}) async-start(), calls=%async_computation | async-start | bytes 3194880 | tf_op jit(solution)/shard_map/all_gather | solution.py:124
  8.9 37.9 %copy-start.4 = (f32[13]{0:T(128)S(1)}, f32[13]{0:T(128)}, u32[]{:S(2)}) copy-start(f32[13]{0:T(128)} %param.9) | copy-start | bytes 160
  8.9 37.9 %copy-start.6 = (s32[1,8]{1,0:T(1,128)S(1)}, s32[1,8]{1,0:T(1,128)}, u32[]{:S(2)}) copy-start(s32[1,8]{1,0:T(1,128)} %param.13) | copy-start | bytes 100
  8.9 79.2 %copy-start.1 = (f32[2,13,48,128]{3,2,1,0:T(8,128)S(1)}, f32[2,13,48,128]{3,2,1,0:T(8,128)}, u32[]{:S(2)}) copy-start(f32[2,13,48,128]{3,2,1,0:T(8,128)} %param.8) | copy-start | bytes 1916932
  10.9 77.6 %copy-start.2 = (s32[48,128]{1,0:T(8,128)S(1)}, s32[48,128]{1,0:T(8,128)}, u32[]{:S(2)}) copy-start(s32[48,128]{1,0:T(8,128)} %param.10) | copy-start | bytes 73732
  11.8 35.1 %collective-permute-start = (f32[2,13,356]{2,0,1:T(2,128)S(1)}, f32[2,13,356]{2,0,1:T(2,128)S(1)}, u32[]{:S(2)}, u32[]{:S(2)}) collective-permute-start(f32[2,13,356]{2,0,1:T(2,128)S(1)} %concatenate.58), channel_id=1, source_target_pairs={{0,4},{4,8},{8,12},{12,16},{16,20},{20,24},{24,28},{28,32},{32,36}... | collective-permute-start | bytes 111080 | tf_op jit(solution)/shard_map/ppermute | solution.py:13
  15.7 33.1 %collective-permute-start.1 = (f32[2,13,356]{2,0,1:T(2,128)S(1)}, f32[2,13,356]{2,0,1:T(2,128)S(1)}, u32[]{:S(2)}, u32[]{:S(2)}) collective-permute-start(f32[2,13,356]{2,0,1:T(2,128)S(1)} %concatenate.58), channel_id=1, source_target_pairs={{0,60},{4,64},{8,68},{12,72},{16,76},{20,80},{24,84},{28,88},{32,9... | collective-permute-start | bytes 111080 | tf_op jit(solution)/shard_map/ppermute | solution.py:13
  24.2 31.8 %collective-permute-start.2 = (f32[2,13,356]{2,0,1:T(2,128)S(1)}, f32[2,13,356]{2,0,1:T(2,128)S(1)}, u32[]{:S(2)}, u32[]{:S(2)}) collective-permute-start(f32[2,13,356]{2,0,1:T(2,128)S(1)} %concatenate.58), channel_id=1, source_target_pairs={{0,64},{4,68},{8,72},{12,76},{16,80},{20,84},{24,88},{28,92},{32,9... | collective-permute-start | bytes 111080 | tf_op jit(solution)/shard_map/ppermute | solution.py:13
  30.4 29.7 %collective-permute-start.3 = (f32[2,13,356]{2,0,1:T(2,128)S(1)}, f32[2,13,356]{2,0,1:T(2,128)S(1)}, u32[]{:S(2)}, u32[]{:S(2)}) collective-permute-start(f32[2,13,356]{2,0,1:T(2,128)S(1)} %concatenate.58), channel_id=1, source_target_pairs={{0,68},{4,72},{8,76},{12,80},{16,84},{20,88},{24,92},{28,96},{32,1... | collective-permute-start | bytes 111080 | tf_op jit(solution)/shard_map/ppermute | solution.py:13
  32.6 29.4 %collective-permute-start.4 = (f32[2,13,356]{2,0,1:T(2,128)S(1)}, f32[2,13,356]{2,0,1:T(2,128)S(1)}, u32[]{:S(2)}, u32[]{:S(2)}) collective-permute-start(f32[2,13,356]{2,0,1:T(2,128)S(1)} %concatenate.58), channel_id=1, source_target_pairs={{0,124},{4,128},{8,132},{12,136},{16,140},{20,144},{24,148},{28,15... | collective-permute-start | bytes 111080 | tf_op jit(solution)/shard_map/ppermute | solution.py:13
  46.9 41.9 %collective-permute-start.5 = (f32[2,13,356]{2,0,1:T(2,128)S(1)}, f32[2,13,356]{2,0,1:T(2,128)S(1)}, u32[]{:S(2)}, u32[]{:S(2)}) collective-permute-start(f32[2,13,356]{2,0,1:T(2,128)S(1)} %concatenate.58), channel_id=1, source_target_pairs={{0,388},{4,392},{8,396},{12,400},{16,404},{20,408},{24,412},{28,41... | collective-permute-start | bytes 111080 | tf_op jit(solution)/shard_map/ppermute | solution.py:13
  48.8 40.0 %collective-permute-start.6 = (f32[2,13,356]{2,0,1:T(2,128)S(1)}, f32[2,13,356]{2,0,1:T(2,128)S(1)}, u32[]{:S(2)}, u32[]{:S(2)}) collective-permute-start(f32[2,13,356]{2,0,1:T(2,128)S(1)} %concatenate.58), channel_id=1, source_target_pairs={{0,444},{4,448},{8,452},{12,456},{16,460},{20,464},{24,468},{28,47... | collective-permute-start | bytes 111080 | tf_op jit(solution)/shard_map/ppermute | solution.py:13
  56.1 32.8 %collective-permute-start.7 = (f32[2,13,356]{2,0,1:T(2,128)S(1)}, f32[2,13,356]{2,0,1:T(2,128)S(1)}, u32[]{:S(2)}, u32[]{:S(2)}) collective-permute-start(f32[2,13,356]{2,0,1:T(2,128)S(1)} %concatenate.58), channel_id=1, source_target_pairs={{0,448},{4,452},{8,456},{12,460},{16,464},{20,468},{24,472},{28,47... | collective-permute-start | bytes 111080 | tf_op jit(solution)/shard_map/ppermute | solution.py:13
  60.1 28.9 %collective-permute-start.8 = (f32[2,13,356]{2,0,1:T(2,128)S(1)}, f32[2,13,356]{2,0,1:T(2,128)S(1)}, u32[]{:S(2)}, u32[]{:S(2)}) collective-permute-start(f32[2,13,356]{2,0,1:T(2,128)S(1)} %concatenate.58), channel_id=1, source_target_pairs={{0,452},{4,456},{8,460},{12,464},{16,468},{20,472},{24,476},{28,48... | collective-permute-start | bytes 111080 | tf_op jit(solution)/shard_map/ppermute | solution.py:13
  62.0 27.0 %collective-permute-start.9 = (f32[2,13,356]{2,0,1:T(2,128)S(1)}, f32[2,13,356]{2,0,1:T(2,128)S(1)}, u32[]{:S(2)}, u32[]{:S(2)}) collective-permute-start(f32[2,13,356]{2,0,1:T(2,128)S(1)} %concatenate.58), channel_id=1, source_target_pairs={{0,508},{4,0},{8,4},{12,8},{16,12},{20,16},{24,20},{28,24},{32,28}... | collective-permute-start | bytes 111080 | tf_op jit(solution)/shard_map/ppermute | solution.py:13
  88.1 1.8 copy-start.5
  95.7 1.6 copy-start.3
  96.8 152.0 %all-gather.5.cloned.1.call-start = ((), (), s32[]{:S(2)}) async-start(), calls=%async_computation.1 | async-start | bytes 3194880 | tf_op jit(solution)/shard_map/all_gather | solution.py:124
  142.0 30.6 %collective-permute-start.10 = (f32[2,13,356]{2,1,0:T(8,128)S(1)}, f32[2,13,356]{2,1,0:T(8,128)S(1)}, u32[]{:S(2)}, u32[]{:S(2)}) collective-permute-start(f32[2,13,356]{2,1,0:T(8,128)S(1)} %concatenate.66), channel_id=1, source_target_pairs={{0,4},{4,8},{8,12},{12,16},{16,20},{20,24},{24,28},{28,32},{32,36}... | collective-permute-start | bytes 111080 | tf_op jit(solution)/shard_map/ppermute | solution.py:13
  145.1 29.4 %collective-permute-start.11 = (f32[2,13,356]{2,1,0:T(8,128)S(1)}, f32[2,13,356]{2,1,0:T(8,128)S(1)}, u32[]{:S(2)}, u32[]{:S(2)}) collective-permute-start(f32[2,13,356]{2,1,0:T(8,128)S(1)} %concatenate.66), channel_id=1, source_target_pairs={{0,60},{4,64},{8,68},{12,72},{16,76},{20,80},{24,84},{28,88},{32,9... | collective-permute-start | bytes 111080 | tf_op jit(solution)/shard_map/ppermute | solution.py:13
  152.9 31.1 %collective-permute-start.12 = (f32[2,13,356]{2,1,0:T(8,128)S(1)}, f32[2,13,356]{2,1,0:T(8,128)S(1)}, u32[]{:S(2)}, u32[]{:S(2)}) collective-permute-start(f32[2,13,356]{2,1,0:T(8,128)S(1)} %concatenate.66), channel_id=1, source_target_pairs={{0,64},{4,68},{8,72},{12,76},{16,80},{20,84},{24,88},{28,92},{32,9... | collective-permute-start | bytes 111080 | tf_op jit(solution)/shard_map/ppermute | solution.py:13
  158.3 27.6 %collective-permute-start.13 = (f32[2,13,356]{2,1,0:T(8,128)S(1)}, f32[2,13,356]{2,1,0:T(8,128)S(1)}, u32[]{:S(2)}, u32[]{:S(2)}) collective-permute-start(f32[2,13,356]{2,1,0:T(8,128)S(1)} %concatenate.66), channel_id=1, source_target_pairs={{0,68},{4,72},{8,76},{12,80},{16,84},{20,88},{24,92},{28,96},{32,1... | collective-permute-start | bytes 111080 | tf_op jit(solution)/shard_map/ppermute | solution.py:13
  160.2 27.7 %collective-permute-start.14 = (f32[2,13,356]{2,1,0:T(8,128)S(1)}, f32[2,13,356]{2,1,0:T(8,128)S(1)}, u32[]{:S(2)}, u32[]{:S(2)}) collective-permute-start(f32[2,13,356]{2,1,0:T(8,128)S(1)} %concatenate.66), channel_id=1, source_target_pairs={{0,124},{4,128},{8,132},{12,136},{16,140},{20,144},{24,148},{28,15... | collective-permute-start | bytes 111080 | tf_op jit(solution)/shard_map/ppermute | solution.py:13
  172.6 23.5 %collective-permute-start.15 = (f32[2,13,356]{2,1,0:T(8,128)S(1)}, f32[2,13,356]{2,1,0:T(8,128)S(1)}, u32[]{:S(2)}, u32[]{:S(2)}) collective-permute-start(f32[2,13,356]{2,1,0:T(8,128)S(1)} %concatenate.66), channel_id=1, source_target_pairs={{0,388},{4,392},{8,396},{12,400},{16,404},{20,408},{24,412},{28,41... | collective-permute-start | bytes 111080 | tf_op jit(solution)/shard_map/ppermute | solution.py:13
  174.5 21.5 %collective-permute-start.16 = (f32[2,13,356]{2,1,0:T(8,128)S(1)}, f32[2,13,356]{2,1,0:T(8,128)S(1)}, u32[]{:S(2)}, u32[]{:S(2)}) collective-permute-start(f32[2,13,356]{2,1,0:T(8,128)S(1)} %concatenate.66), channel_id=1, source_target_pairs={{0,444},{4,448},{8,452},{12,456},{16,460},{20,464},{24,468},{28,47... | collective-permute-start | bytes 111080 | tf_op jit(solution)/shard_map/ppermute | solution.py:13
  184.0 12.1 %collective-permute-start.17 = (f32[2,13,356]{2,1,0:T(8,128)S(1)}, f32[2,13,356]{2,1,0:T(8,128)S(1)}, u32[]{:S(2)}, u32[]{:S(2)}) collective-permute-start(f32[2,13,356]{2,1,0:T(8,128)S(1)} %concatenate.66), channel_id=1, source_target_pairs={{0,448},{4,452},{8,456},{12,460},{16,464},{20,468},{24,472},{28,47... | collective-permute-start | bytes 111080 | tf_op jit(solution)/shard_map/ppermute | solution.py:13
  186.0 10.2 %collective-permute-start.18 = (f32[2,13,356]{2,1,0:T(8,128)S(1)}, f32[2,13,356]{2,1,0:T(8,128)S(1)}, u32[]{:S(2)}, u32[]{:S(2)}) collective-permute-start(f32[2,13,356]{2,1,0:T(8,128)S(1)} %concatenate.66), channel_id=1, source_target_pairs={{0,452},{4,456},{8,460},{12,464},{16,468},{20,472},{24,476},{28,48... | collective-permute-start | bytes 111080 | tf_op jit(solution)/shard_map/ppermute | solution.py:13
  187.9 9.1 %collective-permute-start.19 = (f32[2,13,356]{2,1,0:T(8,128)S(1)}, f32[2,13,356]{2,1,0:T(8,128)S(1)}, u32[]{:S(2)}, u32[]{:S(2)}) collective-permute-start(f32[2,13,356]{2,1,0:T(8,128)S(1)} %concatenate.66), channel_id=1, source_target_pairs={{0,508},{4,0},{8,4},{12,8},{16,12},{20,16},{24,20},{28,24},{32,28}... | collective-permute-start | bytes 111080 | tf_op jit(solution)/shard_map/ppermute | solution.py:13
Sparse Core Ops, SparseCore 0:
  96.9 38.9 all-gather.2
  204.1 44.6 all-gather.4
where the time goes:
time: 263 us; the launch traced here: 262 us
  starting transfers between devices  114 us (43%)
  waiting for transfers between devices  84.3 us (32%)
  between operations  29.8 us (11%)
  local copies, waits for them, and re-layouts  15.7 us (6%)
  matrix products  10.5 us (4%)
  other arithmetic  6.93 us (3%)
    ppermute x20, starting transfers between devices, passed_along(): return lax.ppermute(value, axis, pairs)  114 us
    all_gather x2, waiting for transfers between devices, local(): lax.all_gather(lateral, 'lev', axis=1, tiled=True)  83.4 us
    dot_general x2, matrix products, local(): jnp.einsum('tsml,tmxy->tslxy', own_levels, lax.all_gather(lateral, 'lev',...  9.63 us
  transfers between devices with their start and end apart: 22, of which 3 were waited for; matrix products, arithmetic and copies ran while one was open for 1% of the time, Pallas kernels for 0%

commit v1 on v0

--- a/solution.py
+++ b/solution.py
@@ -121,7 +121,15 @@
         both_states = jnp.einsum(
             "tsml,tmxy->tslxy",
             own_levels,
-            lax.all_gather(lateral, "lev", axis=1, tiled=True),
+            jnp.concatenate(
+                lax.all_to_all(
+                    jnp.stack([lateral for _ in range(lax.psum(1, "lev"))]),
+                    axis_name="lev",
+                    split_axis=0,
+                    concat_axis=0,
+                ),
+                axis=1,
+            ),
             precision=lax.Precision.HIGHEST,
         )
         adjoint = jnp.where(convective[None, None] == 1, both_states[:, 1], both_states[:, 0])

time: 263 us -> 235 us (0.89)
  waiting for transfers between devices: 84.3 us -> 30.5 us
  blocking collectives: 0 us -> 36.6 us
  between operations: 29.8 us -> 16.1 us
  starting transfers between devices: 114 us -> 120 us
  matrix products: 10.5 us -> 5.76 us
    all_gather x2 -> x0, waiting for transfers between devices: 83.4 us -> none  [local(): lax.all_gather(lateral, 'lev', axis=1, tiled=True)]
    all_to_all x0 -> x1, blocking collectives: none -> 36.6 us  [local(): lax.all_to_all(jnp.stack([lateral for _ in range(lax.psum(1, 'lev'))]), a...]
    all_to_all x0 -> x1, waiting for transfers between devices: none -> 29.4 us  [local(): lax.all_to_all(jnp.stack([lateral for _ in range(lax.psum(1, 'lev'))]), a...]
    all_to_all x0 -> x1, starting transfers between devices: none -> 6.94 us  [local(): lax.all_to_all(jnp.stack([lateral for _ in range(lax.psum(1, 'lev'))]), a...]
    dot_general x2, matrix products: 9.63 us -> 4.83 us  [local(): jnp.einsum('tsml,tmxy->tslxy', own_levels, jnp.concatenate(lax.all_to_all...]
  transfers between devices with their start and end apart: 22 -> 21, of which waited for: 3 -> 2; matrix products, arithmetic and copies ran while one was open for 1% -> 1% of each run, Pallas kernels for 0% -> 0%
where the time goes in v1:
time: 235 us; the launch traced here: 232 us
  starting transfers between devices  120 us (51%)
  blocking collectives  36.6 us (16%)
  waiting for transfers between devices  30.5 us (13%)
  local copies, waits for them, and re-layouts  16.3 us (7%)
  between operations  16.1 us (7%)
  other arithmetic  6.93 us (3%)
  matrix products  5.76 us (2%)
    ppermute x20, starting transfers between devices, passed_along(): return lax.ppermute(value, axis, pairs)  113 us
    all_to_all x1, blocking collectives, local(): lax.all_to_all(jnp.stack([lateral for _ in range(lax.psum(1, 'lev'))]), a...  36.6 us
    all_to_all x1, waiting for transfers between devices, local(): lax.all_to_all(jnp.stack([lateral for _ in range(lax.psum(1, 'lev'))]), a...  29.4 us
    all_to_all x1, starting transfers between devices, local(): lax.all_to_all(jnp.stack([lateral for _ in range(lax.psum(1, 'lev'))]), a...  6.94 us
    dot_general x2, matrix products, local(): jnp.einsum('tsml,tmxy->tslxy', own_levels, jnp.concatenate(lax.all_to_all...  4.83 us
  transfers between devices with their start and end apart: 21, of which 2 were waited for; matrix products, arithmetic and copies ran while one was open for 1% of the time, Pallas kernels for 0%

profile of v1, /device:TPU:1, one launch (start us, length us, event | category | flops | bytes accessed | tf_op | source)
XLA Modules:
  0.0 232.2 jit_solution(13351951830591135667)
XLA Ops:
  0.0 1.0 fusion.37
  1.0 1.4 slice_reduce_fusion
  2.4 1.6 fusion.36
  4.4 0.3 copy.903
  4.7 0.3 copy.904
  5.1 0.2 concatenate.58
  5.3 3.9 %collective-permute-start = (f32[2,13,356]{2,0,1:T(2,128)S(1)}, f32[2,13,356]{2,0,1:T(2,128)S(1)}, u32[]{:S(2)}, u32[]{:S(2)}) collective-permute-start(f32[2,13,356]{2,0,1:T(2,128)S(1)} %concatenate.58), channel_id=1, source_target_pairs={{0,4},{4,8},{8,12},{12,16},{16,20},{20,24},{24,28},{28,32},{32,36}... | collective-permute-start | bytes 111080 | tf_op jit(solution)/shard_map/ppermute | solution.py:13
  9.2 8.5 %collective-permute-start.1 = (f32[2,13,356]{2,0,1:T(2,128)S(1)}, f32[2,13,356]{2,0,1:T(2,128)S(1)}, u32[]{:S(2)}, u32[]{:S(2)}) collective-permute-start(f32[2,13,356]{2,0,1:T(2,128)S(1)} %concatenate.58), channel_id=1, source_target_pairs={{0,60},{4,64},{8,68},{12,72},{16,76},{20,80},{24,84},{28,88},{32,9... | collective-permute-start | bytes 111080 | tf_op jit(solution)/shard_map/ppermute | solution.py:13
  17.7 6.1 %collective-permute-start.2 = (f32[2,13,356]{2,0,1:T(2,128)S(1)}, f32[2,13,356]{2,0,1:T(2,128)S(1)}, u32[]{:S(2)}, u32[]{:S(2)}) collective-permute-start(f32[2,13,356]{2,0,1:T(2,128)S(1)} %concatenate.58), channel_id=1, source_target_pairs={{0,64},{4,68},{8,72},{12,76},{16,80},{20,84},{24,88},{28,92},{32,9... | collective-permute-start | bytes 111080 | tf_op jit(solution)/shard_map/ppermute | solution.py:13
  23.8 2.2 collective-permute-start.3
  26.0 14.2 %collective-permute-start.4 = (f32[2,13,356]{2,0,1:T(2,128)S(1)}, f32[2,13,356]{2,0,1:T(2,128)S(1)}, u32[]{:S(2)}, u32[]{:S(2)}) collective-permute-start(f32[2,13,356]{2,0,1:T(2,128)S(1)} %concatenate.58), channel_id=1, source_target_pairs={{0,124},{4,128},{8,132},{12,136},{16,140},{20,144},{24,148},{28,15... | collective-permute-start | bytes 111080 | tf_op jit(solution)/shard_map/ppermute | solution.py:13
  40.3 1.9 collective-permute-start.5
  42.3 7.3 %collective-permute-start.6 = (f32[2,13,356]{2,0,1:T(2,128)S(1)}, f32[2,13,356]{2,0,1:T(2,128)S(1)}, u32[]{:S(2)}, u32[]{:S(2)}) collective-permute-start(f32[2,13,356]{2,0,1:T(2,128)S(1)} %concatenate.58), channel_id=1, source_target_pairs={{0,444},{4,448},{8,452},{12,456},{16,460},{20,464},{24,468},{28,47... | collective-permute-start | bytes 111080 | tf_op jit(solution)/shard_map/ppermute | solution.py:13
  49.6 4.0 %collective-permute-start.7 = (f32[2,13,356]{2,0,1:T(2,128)S(1)}, f32[2,13,356]{2,0,1:T(2,128)S(1)}, u32[]{:S(2)}, u32[]{:S(2)}) collective-permute-start(f32[2,13,356]{2,0,1:T(2,128)S(1)} %concatenate.58), channel_id=1, source_target_pairs={{0,448},{4,452},{8,456},{12,460},{16,464},{20,468},{24,472},{28,47... | collective-permute-start | bytes 111080 | tf_op jit(solution)/shard_map/ppermute | solution.py:13
  53.5 1.9 collective-permute-start.8
  55.5 10.3 %collective-permute-start.9 = (f32[2,13,356]{2,0,1:T(2,128)S(1)}, f32[2,13,356]{2,0,1:T(2,128)S(1)}, u32[]{:S(2)}, u32[]{:S(2)}) collective-permute-start(f32[2,13,356]{2,0,1:T(2,128)S(1)} %concatenate.58), channel_id=1, source_target_pairs={{0,508},{4,0},{8,4},{12,8},{16,12},{20,16},{24,20},{28,24},{32,28}... | collective-permute-start | bytes 111080 | tf_op jit(solution)/shard_map/ppermute | solution.py:13
  65.7 0.7 fusion.42
  81.3 0.2 copy.900
  82.2 0.8 stack.90
  83.0 0.4 fusion.26
  83.4 0.2 fusion.39
  84.4 0.1 rev.25
  84.6 0.4 copy.926
  85.2 0.1 rev.26
  85.4 0.4 copy.928
  86.0 1.3 maximum_maximum_fusion
  87.3 1.5 fusion.16
  88.9 0.2 copy.938
  89.1 1.7 stack.91
  90.8 6.9 %all-to-all-start = ((f32[4,2,13,48,128]{4,3,2,1,0:T(8,128)}), f32[4,2,13,48,128]{4,3,2,1,0:T(8,128)S(1)}, u32[]{:S(2)}, u32[]{:S(2)}) async-start(f32[4,2,13,48,128]{4,3,2,1,0:T(8,128)} %stack.91), calls=%async_computation | async-start | bytes 5111808 | tf_op jit(solution)/shard_map/all_to_all | solution.py:125
  97.7 0.2 constant_dynamic-slice_fusion.8
  97.9 0.1 copy.987
  98.1 29.4 %all-to-all-done = f32[4,2,13,48,128]{4,3,2,1,0:T(8,128)S(1)} async-done(((f32[4,2,13,48,128]{4,3,2,1,0:T(8,128)}), f32[4,2,13,48,128]{4,3,2,1,0:T(8,128)S(1)}, u32[]{:S(2)}, u32[]{:S(2)}) %all-to-all-start) | async-done | bytes 2555936 | tf_op jit(solution)/shard_map/all_to_all | solution.py:125
  127.5 0.2 copy.939
  127.7 2.4 %fusion.2 = f32[2,2,13,48,128]{4,2,3,1,0:T(8,128)S(1)} fusion(f32[2,52,48,128,1]{3,2,1,0,4:T(8,128)S(1)} %bitcast.199, f32[2,2,52,13]{2,3,1,0:T(8,128)S(1)} %copy.987), kind=kOutput, calls=%fused_computation.2 | convolution fusion | flops 199360512 | bytes 3844672 | tf_op jit(solution)/shard_map/tsml,tmxy->tslxy/dot_general | solution.py:121
  130.1 0.1 fusion.13
  130.2 0.3 fusion.35
  130.6 0.4 copy.943
  130.9 0.3 copy.944
  131.4 1.9 collective-permute-start.10
  133.3 5.2 %collective-permute-start.11 = (f32[2,13,356]{2,1,0:T(8,128)S(1)}, f32[2,13,356]{2,1,0:T(8,128)S(1)}, u32[]{:S(2)}, u32[]{:S(2)}) collective-permute-start(f32[2,13,356]{2,1,0:T(8,128)S(1)} %concatenate.66), channel_id=1, source_target_pairs={{0,60},{4,64},{8,68},{12,72},{16,76},{20,80},{24,84},{28,88},{32,9... | collective-permute-start | bytes 111080 | tf_op jit(solution)/shard_map/ppermute | solution.py:13
  138.5 4.0 %collective-permute-start.12 = (f32[2,13,356]{2,1,0:T(8,128)S(1)}, f32[2,13,356]{2,1,0:T(8,128)S(1)}, u32[]{:S(2)}, u32[]{:S(2)}) collective-permute-start(f32[2,13,356]{2,1,0:T(8,128)S(1)} %concatenate.66), channel_id=1, source_target_pairs={{0,64},{4,68},{8,72},{12,76},{16,80},{20,84},{24,88},{28,92},{32,9... | collective-permute-start | bytes 111080 | tf_op jit(solution)/shard_map/ppermute | solution.py:13
  142.5 1.9 collective-permute-start.13
  144.5 13.5 %collective-permute-start.14 = (f32[2,13,356]{2,1,0:T(8,128)S(1)}, f32[2,13,356]{2,1,0:T(8,128)S(1)}, u32[]{:S(2)}, u32[]{:S(2)}) collective-permute-start(f32[2,13,356]{2,1,0:T(8,128)S(1)} %concatenate.66), channel_id=1, source_target_pairs={{0,124},{4,128},{8,132},{12,136},{16,140},{20,144},{24,148},{28,15... | collective-permute-start | bytes 111080 | tf_op jit(solution)/shard_map/ppermute | solution.py:13
  158.0 1.9 collective-permute-start.15
  160.0 8.4 %collective-permute-start.16 = (f32[2,13,356]{2,1,0:T(8,128)S(1)}, f32[2,13,356]{2,1,0:T(8,128)S(1)}, u32[]{:S(2)}, u32[]{:S(2)}) collective-permute-start(f32[2,13,356]{2,1,0:T(8,128)S(1)} %concatenate.66), channel_id=1, source_target_pairs={{0,444},{4,448},{8,452},{12,456},{16,460},{20,464},{24,468},{28,47... | collective-permute-start | bytes 111080 | tf_op jit(solution)/shard_map/ppermute | solution.py:13
  168.4 3.7 %collective-permute-start.17 = (f32[2,13,356]{2,1,0:T(8,128)S(1)}, f32[2,13,356]{2,1,0:T(8,128)S(1)}, u32[]{:S(2)}, u32[]{:S(2)}) collective-permute-start(f32[2,13,356]{2,1,0:T(8,128)S(1)} %concatenate.66), channel_id=1, source_target_pairs={{0,448},{4,452},{8,456},{12,460},{16,464},{20,468},{24,472},{28,47... | collective-permute-start | bytes 111080 | tf_op jit(solution)/shard_map/ppermute | solution.py:13
  172.1 1.9 collective-permute-start.18
  174.1 10.3 %collective-permute-start.19 = (f32[2,13,356]{2,1,0:T(8,128)S(1)}, f32[2,13,356]{2,1,0:T(8,128)S(1)}, u32[]{:S(2)}, u32[]{:S(2)}) collective-permute-start(f32[2,13,356]{2,1,0:T(8,128)S(1)} %concatenate.66), channel_id=1, source_target_pairs={{0,508},{4,0},{8,4},{12,8},{16,12},{20,16},{24,20},{28,24},{32,28}... | collective-permute-start | bytes 111080 | tf_op jit(solution)/shard_map/ppermute | solution.py:13
  184.5 1.0 collective-permute-done.19
  185.5 0.6 fusion.21
  186.1 0.2 fusion.38
  187.1 0.1 rev.29
  187.3 0.4 copy.957
  188.0 0.4 copy.958
  188.6 1.3 maximum_maximum_fusion.1
  189.9 1.5 fusion.8
  191.5 0.2 copy.966
  191.7 0.2 stack.103
  191.9 36.6 %all_to_all.10 = f32[4,2,13,48,128]{4,3,2,1,0:T(8,128)S(1)} all-to-all(f32[4,2,13,48,128]{4,3,2,1,0:T(8,128)S(1)} %stack.103), channel_id=1, replica_groups=mesh['tile'=128,'lev'=4] {'lev'}, dimensions={0} | all-to-all | bytes 5111808 | tf_op jit(solution)/shard_map/all_to_all | solution.py:125
  228.5 0.2 copy.967
  228.7 2.4 %fusion = f32[2,2,13,48,128]{4,2,3,0,1:T(8,128)S(1)} fusion(f32[2,52,48,128]{3,2,1,0:T(8,128)S(1)} %bitcast.198, f32[2,2,52,13]{2,3,1,0:T(8,128)S(1)} %copy.987), kind=kOutput, calls=%fused_computation | convolution fusion | flops 199360512 | bytes 3844672 | tf_op jit(solution)/shard_map/tsml,tmxy->tslxy/dot_general | solution.py:121
  231.1 0.1 fusion.5
  231.2 1.0 copy.971
  (118 shorter events, 3.5 us)
Async XLA Ops:
  0.0 97.7 %copy-start = (f32[2,2,52,52]{3,1,2,0:T(2,128)S(1)}, f32[2,2,52,52]{3,1,2,0:T(2,128)}, u32[]{:S(2)}) copy-start(f32[2,2,52,52]{3,1,2,0:T(2,128)} %param.12) | copy-start | bytes 129796
  2.4 37.9 %copy-start.4 = (f32[13]{0:T(128)S(1)}, f32[13]{0:T(128)}, u32[]{:S(2)}) copy-start(f32[13]{0:T(128)} %param.9) | copy-start | bytes 160
  2.4 37.9 %copy-start.6 = (s32[1,8]{1,0:T(1,128)S(1)}, s32[1,8]{1,0:T(1,128)}, u32[]{:S(2)}) copy-start(s32[1,8]{1,0:T(1,128)} %param.13) | copy-start | bytes 100
  2.4 78.8 %copy-start.1 = (f32[2,13,48,128]{3,2,1,0:T(8,128)S(1)}, f32[2,13,48,128]{3,2,1,0:T(8,128)}, u32[]{:S(2)}) copy-start(f32[2,13,48,128]{3,2,1,0:T(8,128)} %param.8) | copy-start | bytes 1916932
  4.3 77.3 %copy-start.2 = (s32[48,128]{1,0:T(8,128)S(1)}, s32[48,128]{1,0:T(8,128)}, u32[]{:S(2)}) copy-start(s32[48,128]{1,0:T(8,128)} %param.10) | copy-start | bytes 73732
  5.3 35.1 %collective-permute-start = (f32[2,13,356]{2,0,1:T(2,128)S(1)}, f32[2,13,356]{2,0,1:T(2,128)S(1)}, u32[]{:S(2)}, u32[]{:S(2)}) collective-permute-start(f32[2,13,356]{2,0,1:T(2,128)S(1)} %concatenate.58), channel_id=1, source_target_pairs={{0,4},{4,8},{8,12},{12,16},{16,20},{20,24},{24,28},{28,32},{32,36}... | collective-permute-start | bytes 111080 | tf_op jit(solution)/shard_map/ppermute | solution.py:13
  9.2 33.1 %collective-permute-start.1 = (f32[2,13,356]{2,0,1:T(2,128)S(1)}, f32[2,13,356]{2,0,1:T(2,128)S(1)}, u32[]{:S(2)}, u32[]{:S(2)}) collective-permute-start(f32[2,13,356]{2,0,1:T(2,128)S(1)} %concatenate.58), channel_id=1, source_target_pairs={{0,60},{4,64},{8,68},{12,72},{16,76},{20,80},{24,84},{28,88},{32,9... | collective-permute-start | bytes 111080 | tf_op jit(solution)/shard_map/ppermute | solution.py:13
  17.7 31.8 %collective-permute-start.2 = (f32[2,13,356]{2,0,1:T(2,128)S(1)}, f32[2,13,356]{2,0,1:T(2,128)S(1)}, u32[]{:S(2)}, u32[]{:S(2)}) collective-permute-start(f32[2,13,356]{2,0,1:T(2,128)S(1)} %concatenate.58), channel_id=1, source_target_pairs={{0,64},{4,68},{8,72},{12,76},{16,80},{20,84},{24,88},{28,92},{32,9... | collective-permute-start | bytes 111080 | tf_op jit(solution)/shard_map/ppermute | solution.py:13
  23.8 29.7 %collective-permute-start.3 = (f32[2,13,356]{2,0,1:T(2,128)S(1)}, f32[2,13,356]{2,0,1:T(2,128)S(1)}, u32[]{:S(2)}, u32[]{:S(2)}) collective-permute-start(f32[2,13,356]{2,0,1:T(2,128)S(1)} %concatenate.58), channel_id=1, source_target_pairs={{0,68},{4,72},{8,76},{12,80},{16,84},{20,88},{24,92},{28,96},{32,1... | collective-permute-start | bytes 111080 | tf_op jit(solution)/shard_map/ppermute | solution.py:13
  26.0 29.4 %collective-permute-start.4 = (f32[2,13,356]{2,0,1:T(2,128)S(1)}, f32[2,13,356]{2,0,1:T(2,128)S(1)}, u32[]{:S(2)}, u32[]{:S(2)}) collective-permute-start(f32[2,13,356]{2,0,1:T(2,128)S(1)} %concatenate.58), channel_id=1, source_target_pairs={{0,124},{4,128},{8,132},{12,136},{16,140},{20,144},{24,148},{28,15... | collective-permute-start | bytes 111080 | tf_op jit(solution)/shard_map/ppermute | solution.py:13
  40.3 41.6 %collective-permute-start.5 = (f32[2,13,356]{2,0,1:T(2,128)S(1)}, f32[2,13,356]{2,0,1:T(2,128)S(1)}, u32[]{:S(2)}, u32[]{:S(2)}) collective-permute-start(f32[2,13,356]{2,0,1:T(2,128)S(1)} %concatenate.58), channel_id=1, source_target_pairs={{0,388},{4,392},{8,396},{12,400},{16,404},{20,408},{24,412},{28,41... | collective-permute-start | bytes 111080 | tf_op jit(solution)/shard_map/ppermute | solution.py:13
  42.3 39.7 %collective-permute-start.6 = (f32[2,13,356]{2,0,1:T(2,128)S(1)}, f32[2,13,356]{2,0,1:T(2,128)S(1)}, u32[]{:S(2)}, u32[]{:S(2)}) collective-permute-start(f32[2,13,356]{2,0,1:T(2,128)S(1)} %concatenate.58), channel_id=1, source_target_pairs={{0,444},{4,448},{8,452},{12,456},{16,460},{20,464},{24,468},{28,47... | collective-permute-start | bytes 111080 | tf_op jit(solution)/shard_map/ppermute | solution.py:13
  49.6 32.5 %collective-permute-start.7 = (f32[2,13,356]{2,0,1:T(2,128)S(1)}, f32[2,13,356]{2,0,1:T(2,128)S(1)}, u32[]{:S(2)}, u32[]{:S(2)}) collective-permute-start(f32[2,13,356]{2,0,1:T(2,128)S(1)} %concatenate.58), channel_id=1, source_target_pairs={{0,448},{4,452},{8,456},{12,460},{16,464},{20,468},{24,472},{28,47... | collective-permute-start | bytes 111080 | tf_op jit(solution)/shard_map/ppermute | solution.py:13
  53.5 28.6 %collective-permute-start.8 = (f32[2,13,356]{2,0,1:T(2,128)S(1)}, f32[2,13,356]{2,0,1:T(2,128)S(1)}, u32[]{:S(2)}, u32[]{:S(2)}) collective-permute-start(f32[2,13,356]{2,0,1:T(2,128)S(1)} %concatenate.58), channel_id=1, source_target_pairs={{0,452},{4,456},{8,460},{12,464},{16,468},{20,472},{24,476},{28,48... | collective-permute-start | bytes 111080 | tf_op jit(solution)/shard_map/ppermute | solution.py:13
  55.5 26.7 %collective-permute-start.9 = (f32[2,13,356]{2,0,1:T(2,128)S(1)}, f32[2,13,356]{2,0,1:T(2,128)S(1)}, u32[]{:S(2)}, u32[]{:S(2)}) collective-permute-start(f32[2,13,356]{2,0,1:T(2,128)S(1)} %concatenate.58), channel_id=1, source_target_pairs={{0,508},{4,0},{8,4},{12,8},{16,12},{20,16},{24,20},{28,24},{32,28}... | collective-permute-start | bytes 111080 | tf_op jit(solution)/shard_map/ppermute | solution.py:13
  81.2 1.8 copy-start.5
  90.8 7.2 %copy-start.3 = (s32[48,128]{1,0:T(8,128)S(1)}, s32[48,128]{1,0:T(8,128)}, u32[]{:S(2)}) copy-start(s32[48,128]{1,0:T(8,128)} %param.11) | copy-start | bytes 73732
  90.8 36.7 %all-to-all-start = ((f32[4,2,13,48,128]{4,3,2,1,0:T(8,128)}), f32[4,2,13,48,128]{4,3,2,1,0:T(8,128)S(1)}, u32[]{:S(2)}, u32[]{:S(2)}) async-start(f32[4,2,13,48,128]{4,3,2,1,0:T(8,128)} %stack.91), calls=%async_computation | async-start | bytes 5111808 | tf_op jit(solution)/shard_map/all_to_all | solution.py:125
  131.4 26.6 %collective-permute-start.10 = (f32[2,13,356]{2,1,0:T(8,128)S(1)}, f32[2,13,356]{2,1,0:T(8,128)S(1)}, u32[]{:S(2)}, u32[]{:S(2)}) collective-permute-start(f32[2,13,356]{2,1,0:T(8,128)S(1)} %concatenate.66), channel_id=1, source_target_pairs={{0,4},{4,8},{8,12},{12,16},{16,20},{20,24},{24,28},{28,32},{32,36}... | collective-permute-start | bytes 111080 | tf_op jit(solution)/shard_map/ppermute | solution.py:13
  133.3 26.6 %collective-permute-start.11 = (f32[2,13,356]{2,1,0:T(8,128)S(1)}, f32[2,13,356]{2,1,0:T(8,128)S(1)}, u32[]{:S(2)}, u32[]{:S(2)}) collective-permute-start(f32[2,13,356]{2,1,0:T(8,128)S(1)} %concatenate.66), channel_id=1, source_target_pairs={{0,60},{4,64},{8,68},{12,72},{16,76},{20,80},{24,84},{28,88},{32,9... | collective-permute-start | bytes 111080 | tf_op jit(solution)/shard_map/ppermute | solution.py:13
  138.5 29.9 %collective-permute-start.12 = (f32[2,13,356]{2,1,0:T(8,128)S(1)}, f32[2,13,356]{2,1,0:T(8,128)S(1)}, u32[]{:S(2)}, u32[]{:S(2)}) collective-permute-start(f32[2,13,356]{2,1,0:T(8,128)S(1)} %concatenate.66), channel_id=1, source_target_pairs={{0,64},{4,68},{8,72},{12,76},{16,80},{20,84},{24,88},{28,92},{32,9... | collective-permute-start | bytes 111080 | tf_op jit(solution)/shard_map/ppermute | solution.py:13
  142.5 29.6 %collective-permute-start.13 = (f32[2,13,356]{2,1,0:T(8,128)S(1)}, f32[2,13,356]{2,1,0:T(8,128)S(1)}, u32[]{:S(2)}, u32[]{:S(2)}) collective-permute-start(f32[2,13,356]{2,1,0:T(8,128)S(1)} %concatenate.66), channel_id=1, source_target_pairs={{0,68},{4,72},{8,76},{12,80},{16,84},{20,88},{24,92},{28,96},{32,1... | collective-permute-start | bytes 111080 | tf_op jit(solution)/shard_map/ppermute | solution.py:13
  144.5 29.6 %collective-permute-start.14 = (f32[2,13,356]{2,1,0:T(8,128)S(1)}, f32[2,13,356]{2,1,0:T(8,128)S(1)}, u32[]{:S(2)}, u32[]{:S(2)}) collective-permute-start(f32[2,13,356]{2,1,0:T(8,128)S(1)} %concatenate.66), channel_id=1, source_target_pairs={{0,124},{4,128},{8,132},{12,136},{16,140},{20,144},{24,148},{28,15... | collective-permute-start | bytes 111080 | tf_op jit(solution)/shard_map/ppermute | solution.py:13
  158.0 26.4 %collective-permute-start.15 = (f32[2,13,356]{2,1,0:T(8,128)S(1)}, f32[2,13,356]{2,1,0:T(8,128)S(1)}, u32[]{:S(2)}, u32[]{:S(2)}) collective-permute-start(f32[2,13,356]{2,1,0:T(8,128)S(1)} %concatenate.66), channel_id=1, source_target_pairs={{0,388},{4,392},{8,396},{12,400},{16,404},{20,408},{24,412},{28,41... | collective-permute-start | bytes 111080 | tf_op jit(solution)/shard_map/ppermute | solution.py:13
  160.0 24.4 %collective-permute-start.16 = (f32[2,13,356]{2,1,0:T(8,128)S(1)}, f32[2,13,356]{2,1,0:T(8,128)S(1)}, u32[]{:S(2)}, u32[]{:S(2)}) collective-permute-start(f32[2,13,356]{2,1,0:T(8,128)S(1)} %concatenate.66), channel_id=1, source_target_pairs={{0,444},{4,448},{8,452},{12,456},{16,460},{20,464},{24,468},{28,47... | collective-permute-start | bytes 111080 | tf_op jit(solution)/shard_map/ppermute | solution.py:13
  168.4 16.0 %collective-permute-start.17 = (f32[2,13,356]{2,1,0:T(8,128)S(1)}, f32[2,13,356]{2,1,0:T(8,128)S(1)}, u32[]{:S(2)}, u32[]{:S(2)}) collective-permute-start(f32[2,13,356]{2,1,0:T(8,128)S(1)} %concatenate.66), channel_id=1, source_target_pairs={{0,448},{4,452},{8,456},{12,460},{16,464},{20,468},{24,472},{28,47... | collective-permute-start | bytes 111080 | tf_op jit(solution)/shard_map/ppermute | solution.py:13
  172.1 12.3 %collective-permute-start.18 = (f32[2,13,356]{2,1,0:T(8,128)S(1)}, f32[2,13,356]{2,1,0:T(8,128)S(1)}, u32[]{:S(2)}, u32[]{:S(2)}) collective-permute-start(f32[2,13,356]{2,1,0:T(8,128)S(1)} %concatenate.66), channel_id=1, source_target_pairs={{0,452},{4,456},{8,460},{12,464},{16,468},{20,472},{24,476},{28,48... | collective-permute-start | bytes 111080 | tf_op jit(solution)/shard_map/ppermute | solution.py:13
  174.1 11.4 %collective-permute-start.19 = (f32[2,13,356]{2,1,0:T(8,128)S(1)}, f32[2,13,356]{2,1,0:T(8,128)S(1)}, u32[]{:S(2)}, u32[]{:S(2)}) collective-permute-start(f32[2,13,356]{2,1,0:T(8,128)S(1)} %concatenate.66), channel_id=1, source_target_pairs={{0,508},{4,0},{8,4},{12,8},{16,12},{20,16},{24,20},{28,24},{32,28}... | collective-permute-start | bytes 111080 | tf_op jit(solution)/shard_map/ppermute | solution.py:13
